TPU v7x, 32 devices: a whole 2x2x4 slice. The times are simulated.
32 devices in a mesh: shard: 4 (over z), rep: 8 (over y, x, core).
Axes of the slice: x: 2, y: 2, z: 4, core: 2. Of those that a mesh axis runs over, the one named last changes fastest.
Arguments:
- grads: bfloat16 [1, 8192, 28672], P(None, 'shard', 'rep'), may hold values from -81 to 81
- seeds: int32 [1], replicated, may hold values from 0 to 999999
Outputs:
- projected: bfloat16 [512, 1, 28672], P('shard', None, 'rep')
All inputs are finite; a program needn't handle non-finite values.
Results may differ from a plain program's by a relative error of at most 0.0056.
Values may be sent and summed in bfloat16 or wider, within the bound.
No kernel may reach another device: no remote copies, remote signals or barrier semaphores. Data moves between devices by JAX's collectives and lax.ppermute only.
A program may use at most 128 MiB of HBM per device.

v0:
```python
import jax
import jax.numpy as jnp
from jax import lax
from jax.sharding import PartitionSpec as P

RANK = 512
mix_first = 668265263
mix_second = -2048144789
mix_third = -1028477387


def sketch_table(seeds, first_row, count, rank):
    rows = first_row + lax.iota(jnp.int32, count)
    columns = lax.iota(jnp.int32, rank)
    counter = rows[:, None] * jnp.int32(rank) + columns[None, :]
    hashed = jnp.bitwise_xor(counter[None, :, :], (seeds * jnp.int32(mix_first))[:, None, None])
    hashed = hashed * jnp.int32(mix_second)
    hashed = jnp.bitwise_xor(hashed, lax.shift_right_logical(hashed, jnp.int32(15)))
    hashed = hashed * jnp.int32(mix_third)
    hashed = jnp.bitwise_xor(hashed, lax.shift_right_logical(hashed, jnp.int32(13)))
    unit = lax.shift_right_logical(hashed, jnp.int32(8)).astype(jnp.float32) * (1.0 / 16777216.0)
    return (2.0 * unit - 1.0).astype(jnp.bfloat16)


def body(grads, seeds):
    mats, depth, width = grads.shape
    rows_whole = lax.all_to_all(grads, "rep", split_axis=1, concat_axis=2, tiled=True)
    block = rows_whole.shape[2] // 8

    def add_block(step, total):
        start = step * block
        table = sketch_table(seeds, start, block, RANK)
        piece = lax.dynamic_slice_in_dim(rows_whole, start, block, 2)
        return total + jnp.einsum("mdc,mcr->dmr", piece, table, preferred_element_type=jnp.float32)

    sketch_rows = lax.fori_loop(
        0, 8, add_block, jnp.zeros((rows_whole.shape[1], mats, RANK), jnp.float32)
    )
    local_gram = jnp.einsum(
        "dmr,dms->mrs",
        sketch_rows,
        sketch_rows,
        precision=lax.Precision.HIGHEST,
        preferred_element_type=jnp.float32,
    )
    gram = lax.psum(local_gram, ("shard", "rep"))
    factor = jnp.linalg.cholesky(gram)
    own_rows = jnp.transpose(sketch_rows, (1, 0, 2))
    basis_rows = lax.linalg.triangular_solve(
        factor, own_rows, left_side=False, lower=True, transpose_a=True
    ).astype(jnp.bfloat16)
    partial_sum = jnp.einsum(
        "mdr,mdc->rmc",
        lax.all_gather(basis_rows, "rep", axis=1, tiled=True),
        grads,
        preferred_element_type=jnp.float32,
    )
    projected = lax.psum_scatter(partial_sum, "shard", scatter_dimension=0, tiled=True)
    return projected.astype(jnp.bfloat16)


def solution(mesh):
    return jax.shard_map(
        body,
        mesh=mesh,
        in_specs=(P(None, "shard", "rep"), P()),
        out_specs=P("shard", None, "rep"),
        check_vma=False,
    )
```

profile of v0, /device:TPU:0, one launch (start us, length us, event | category | flops | bytes accessed | tf_op | source)
XLA Modules:
  0.0 861.6 jit_solution(14677463218900408071)
XLA Ops:
  6.5 26.0 %copy.30 = bf16[1,2048,3584]{2,0,1:T(2,128)(2,1)} copy(bf16[1,2048,3584]{2,1,0:T(8,128)(2,1)} %param.4) | data formatting | bytes 29360128 | tf_op args[0]
  33.1 94.1 %reduce.36 = bf16[2048,3584]{1,0:T(8,128)(2,1)} reduce(bf16[2048,1,3584]{2,1,0:T(2,128)(2,1)} %bitcast.210, bf16[]{:T(256)} %broadcast.502), dimensions={1}, to_apply=%bitcast.195.reduce_sub_computation | reduce | bytes 29360130
  127.2 16.3 %reshape.459 = bf16[8,2,458752]{2,1,0:T(2,128)(2,1)} reshape(bf16[2048,3584]{1,0:T(8,128)(2,1)} %reduce.36) | data formatting | bytes 29360128
  143.5 5.6 all-to-all-start
  149.9 161.3 %all-to-all-done = bf16[8,2,458752]{2,1,0:T(2,128)(2,1)} async-done(((bf16[8,2,458752]{2,1,0:T(2,128)(2,1)}), bf16[8,2,458752]{2,1,0:T(2,128)(2,1)}, u32[]{:S(2)}, u32[]{:S(2)}) %all-to-all-start) | async-done | bytes 14680096 | tf_op jit(solution)/shard_map/all_to_all | solution.py:27
  311.2 20.2 %reshape.460 = bf16[2048,1,3584]{2,1,0:T(2,128)(2,1)} reshape(bf16[8,2,458752]{2,1,0:T(2,128)(2,1)} %all-to-all-done) | data formatting | bytes 29360128
  331.4 19.4 %copy.28 = bf16[1,2048,3584]{2,1,0:T(8,128)(2,1)} copy(bf16[1,2048,3584]{2,0,1:T(2,128)(2,1)} %bitcast.211) | data formatting | bytes 29360128
  350.8 18.7 %copy.21 = bf16[1,256,8,3584]{1,3,2,0:T(8,128)(2,1)} copy(bf16[1,256,8,3584]{3,1,2,0:T(8,128)(2,1)} %bitcast.212) | data formatting | bytes 29360128 | tf_op jit(solution)/shard_map/all_to_all | solution.py:27
  369.5 42.8 %while.18 = (s32[]{:T(128)}, f32[256,1,512]{0,2,1:T(8,128)S(1)}, s32[1]{0:T(128)}, bf16[1,256,28672]{1,2,0:T(8,128)(2,1)}, s32[]{:T(128)}, /*index=5*/s32[]{:T(128)}, s32[]{:T(128)}, s32[]{:T(128)}) while((s32[]{:T(128)}, f32[256,1,512]{0,2,1:T(8,128)S(1)}, s32[1]{0:T(128)}, bf16[1,256,28672]{1,2,0:T(8,128)(2,1)}, s32[]{:T(128)}, ...), condition=%wide.region_1.0_spmd.clone, body=%wide.region_0.0_spmd.clone.sunk | while | flops 963648512 | bytes 2912917 | solution.py:36
  380.2 5.3 fusion.77
  390.9 5.3 fusion.77
  414.9 130.6 %all-reduce.3.cloned.1.call-done = f32[1,512,512]{1,2,0:T(8,128)} async-done(((f32[1,512,512]{1,2,0:T(8,128)}), f32[1,512,512]{1,2,0:T(8,128)}) %all-reduce.3.cloned.1.call-update) | async-done | bytes 1048592 | tf_op jit(solution)/shard_map/psum | solution.py:46
  548.5 11.7 %custom-call.34 = f32[1,128,128]{2,1,0:T(8,128)S(1)} custom-call(f32[1,128,128]{2,1,0:T(8,128)S(1)} %cholesky.267), custom_call_target="Cholesky" | custom-call | tf_op jit(solution)/shard_map/jit(cholesky)/cholesky | solution.py:47
  560.3 9.8 %custom-call.35 = f32[1,1,128,128]{2,3,1,0:T(8,128)S(1)} custom-call(f32[1,1,128,128]{3,2,1,0:T(8,128)S(1)} %get-tuple-element.173), custom_call_target="InvertDiagBlocksLowerTriangular" | custom-call | tf_op jit(solution)/shard_map/jit(cholesky)/cholesky | solution.py:47
  570.9 11.7 %custom-call.36 = f32[1,128,128]{2,1,0:T(8,128)S(1)} custom-call(f32[1,128,128]{2,1,0:T(8,128)S(1)} %cholesky.271), custom_call_target="Cholesky" | custom-call | tf_op jit(solution)/shard_map/jit(cholesky)/cholesky | solution.py:47
  582.6 10.2 %custom-call.37 = f32[1,1,128,128]{2,3,1,0:T(8,128)S(1)} custom-call(f32[1,1,128,128]{3,2,1,0:T(8,128)S(1)} %get-tuple-element.170), custom_call_target="InvertDiagBlocksLowerTriangular" | custom-call | tf_op jit(solution)/shard_map/jit(cholesky)/cholesky | solution.py:47
  593.5 11.7 %custom-call.38 = f32[1,128,128]{2,1,0:T(8,128)S(1)} custom-call(f32[1,128,128]{2,1,0:T(8,128)S(1)} %cholesky.276), custom_call_target="Cholesky" | custom-call | tf_op jit(solution)/shard_map/jit(cholesky)/cholesky | solution.py:47
  606.0 9.8 %custom-call.39 = f32[1,1,128,128]{2,3,1,0:T(8,128)S(1)} custom-call(f32[1,1,128,128]{3,2,1,0:T(8,128)S(1)} %get-tuple-element.167), custom_call_target="InvertDiagBlocksLowerTriangular" | custom-call | tf_op jit(solution)/shard_map/jit(cholesky)/cholesky | solution.py:47
  616.4 11.7 %custom-call.40 = f32[1,128,128]{2,1,0:T(8,128)S(1)} custom-call(f32[1,128,128]{2,1,0:T(8,128)S(1)} %fusion.46), custom_call_target="Cholesky" | custom-call | tf_op jit(solution)/shard_map/jit(cholesky)/cholesky | solution.py:47
  632.3 8.1 while.17
  640.4 39.3 %custom-call.41 = f32[1,4,128,128]{2,3,1,0:T(8,128)S(1)} custom-call(f32[1,4,128,128]{3,2,1,0:T(8,128)S(1)} %bitcast.221), custom_call_target="InvertDiagBlocksLowerTriangular" | custom-call | tf_op jit(solution)/shard_map/triangular_solve | solution.py:49
  683.7 27.2 %all-gather.2.cloned.1.call-done = bf16[1,2048,512]{1,2,0:T(8,128)(2,1)} async-done(((bf16[1,256,512]{1,2,0:T(8,128)(2,1)}), bf16[1,2048,512]{1,2,0:T(8,128)(2,1)}) %all-gather.2.cloned.1.call-update) | async-done | bytes 2097168 | tf_op jit(solution)/shard_map/all_gather | solution.py:54
  710.9 13.5 %fusion.31 = f32[512,1,3584]{2,0,1:T(8,128)} fusion(bf16[1,2048,3584]{2,1,0:T(8,128)(2,1)} %param.4, bf16[1,2048,512]{1,2,0:T(8,128)(2,1)} %all-gather.2.cloned.1.call-done), kind=kOutput, calls=%fused_computation.27 | convolution fusion | flops 7516192768 | bytes 24117248 | tf_op jit(solution)/shard_map/mdr,mdc->rmc/dot_general | solution.py:52
  724.4 127.9 %reduce-scatter.2.cloned.1.call-done = f32[128,1,3584]{2,0,1:T(8,128)} async-done(((f32[512,1,3584]{2,0,1:T(8,128)}), f32[128,1,3584]{2,0,1:T(8,128)}) %reduce-scatter.2.cloned.1.call-update) | async-done | bytes 1835024 | tf_op jit(solution)/shard_map/reduce_scatter | solution.py:58
  (68 shorter events, 57.1 us)
Async XLA Ops:
  143.5 167.7 %all-to-all-start = ((bf16[8,2,458752]{2,1,0:T(2,128)(2,1)}), bf16[8,2,458752]{2,1,0:T(2,128)(2,1)}, u32[]{:S(2)}, u32[]{:S(2)}) async-start(bf16[8,2,458752]{2,1,0:T(2,128)(2,1)} %reshape.459), calls=%async_computation | async-start | bytes 29360128 | tf_op jit(solution)/shard_map/all_to_all | solution.py:27
  149.1 396.4 %all-reduce.3.cloned.1.call-start = ((), (), s32[]{:S(2)}) async-start(), calls=%async_computation.2 | async-start | bytes 2097152 | tf_op jit(solution)/shard_map/psum | solution.py:46
  414.4 296.5 %all-gather.2.cloned.1.call-start = ((), (), s32[]{:S(2)}) async-start(), calls=%async_computation.3 | async-start | bytes 2359296 | tf_op jit(solution)/shard_map/all_gather | solution.py:54
  683.6 168.7 %reduce-scatter.2.cloned.1.call-start = ((), (), s32[]{:S(2)}) async-start(), calls=%async_computation.4 | async-start | bytes 9175040 | tf_op jit(solution)/shard_map/reduce_scatter | solution.py:58
Sparse Core Ops, SparseCore 0:
  414.5 130.9 all-reduce.2
  683.8 27.0 all-gather.1
  724.5 127.7 reduce-scatter.1
where the time goes:
time: 869 us; the launch traced here: 862 us
  waiting for transfers between devices  447 us (51%)
  other arithmetic  217 us (25%)
  local copies, waits for them, and re-layouts  111 us (13%)
  matrix products  63 us (7%)
  between operations  16.7 us (2%)
    all_to_all x1, waiting for transfers between devices, body(): lax.all_to_all(grads, 'rep', split_axis=1, concat_axis=2, tiled=True)  161 us
    psum x1, waiting for transfers between devices, body(): gram = lax.psum(local_gram, ('shard', 'rep'))  131 us
    reduce_scatter x1, waiting for transfers between devices, body(): lax.psum_scatter(partial_sum, 'shard', scatter_dimension=0, tiled=True)  128 us
    unnamed x3, other arithmetic  94.1 us
    unnamed x5, local copies, waits for them, and re-layouts  82.4 us
    another operation x14, other arithmetic, body(): factor = jnp.linalg.cholesky(gram)  79 us
    dot_general x8, matrix products, add_block(): jnp.einsum('mdc,mcr->dmr', piece, table, preferred_element_type=jnp.float32)  42.5 us
    another operation x4, other arithmetic, body(): lax.linalg.triangular_solve(factor, own_rows, left_side=False, lower=True...  40.2 us
  transfers between devices with their start and end apart: 4, of which 4 were waited for; matrix products, arithmetic and copies ran while one was open for 0% of the time, Pallas kernels for 0%

commit v1 on v0

--- a/solution.py
+++ b/solution.py
@@ -49,12 +49,43 @@
     basis_rows = lax.linalg.triangular_solve(
         factor, own_rows, left_side=False, lower=True, transpose_a=True
     ).astype(jnp.bfloat16)
+    z1 = jax.lax.psum(1, "rep")
+    carry_out = jax.lax.axis_index("rep")
+    e_next, block_out, local_out = (z1, carry_out, basis_rows.shape[1])
+    samples = tuple(((s, (s + 1) % e_next) for s in range(e_next)))
+    pool = tuple(((s, (s - 1) % e_next) for s in range(e_next)))
+    near = e_next // 2
+    current_value = f_next = basis_rows
     partial_sum = jnp.einsum(
         "mdr,mdc->rmc",
-        lax.all_gather(basis_rows, "rep", axis=1, tiled=True),
-        grads,
+        basis_rows,
+        lax.dynamic_slice_in_dim(grads, block_out * local_out, basis_rows.shape[1], axis=1),
         preferred_element_type=jnp.float32,
     )
+    h = 1
+    while h < near + 1:
+        current_value = jax.lax.ppermute(current_value, "rep", samples)
+        if h < e_next - near:
+            f_next = jax.lax.ppermute(f_next, "rep", pool)
+            oldest = jnp.einsum(
+                "mdr,mdc->rmc",
+                f_next,
+                lax.dynamic_slice_in_dim(
+                    grads, (block_out + h) % e_next * local_out, f_next.shape[1], axis=1
+                ),
+                preferred_element_type=jnp.float32,
+            )
+            partial_sum = partial_sum + oldest
+        vec_out = jnp.einsum(
+            "mdr,mdc->rmc",
+            current_value,
+            lax.dynamic_slice_in_dim(
+                grads, (block_out - h) % e_next * local_out, current_value.shape[1], axis=1
+            ),
+            preferred_element_type=jnp.float32,
+        )
+        partial_sum = partial_sum + vec_out
+        h = h + 1
     projected = lax.psum_scatter(partial_sum, "shard", scatter_dimension=0, tiled=True)
     return projected.astype(jnp.bfloat16)
 

time: 869 us -> 896 us (1.031)
  matrix products: 63 us -> 106 us
  waiting for transfers between devices: 447 us -> 419 us
    dot_general x1 -> x8, matrix products: 13.5 us -> 53.3 us  [the longest x4 33.5 us: body(): jnp.einsum('mdr,mdc->rmc', current_value, lax.dynamic_slice_in_dim(grads,...]
    all_gather x1 -> x0, waiting for transfers between devices: 27.2 us -> none  [body(): lax.all_gather(basis_rows, 'rep', axis=1, tiled=True)]
    unnamed x5 -> x13, local copies, waits for them, and re-layouts: 82.4 us -> 82.4 us
    unnamed x3 -> x4, other arithmetic: 94.1 us -> 94.1 us
  transfers between devices with their start and end apart: 4 -> 10, of which waited for: 4 -> 3; matrix products, arithmetic and copies ran while one was open for 0% -> 4% of each run, Pallas kernels for 0% -> 0%
where the time goes in v1:
time: 896 us; the launch traced here: 889 us
  waiting for transfers between devices  419 us (47%)
  other arithmetic  216 us (24%)
  local copies, waits for them, and re-layouts  116 us (13%)
  matrix products  106 us (12%)
  between operations  17.2 us (2%)
  starting transfers between devices  14.2 us (2%)
    all_to_all x1, waiting for transfers between devices, body(): lax.all_to_all(grads, 'rep', split_axis=1, concat_axis=2, tiled=True)  161 us
    psum x1, waiting for transfers between devices, body(): gram = lax.psum(local_gram, ('shard', 'rep'))  130 us
    reduce_scatter x1, waiting for transfers between devices, body(): lax.psum_scatter(partial_sum, 'shard', scatter_dimension=0, tiled=True)  128 us
    unnamed x4, other arithmetic  94.1 us
    unnamed x13, local copies, waits for them, and re-layouts  82.4 us
    another operation x14, other arithmetic, body(): factor = jnp.linalg.cholesky(gram)  79 us
    dot_general x8, matrix products, add_block(): jnp.einsum('mdc,mcr->dmr', piece, table, preferred_element_type=jnp.float32)  42.5 us
    another operation x4, other arithmetic, body(): lax.linalg.triangular_solve(factor, own_rows, left_side=False, lower=True...  40.3 us
  transfers between devices with their start and end apart: 10, of which 3 were waited for; matrix products, arithmetic and copies ran while one was open for 4% of the time, Pallas kernels for 0%

profile of v1, /device:TPU:0, one launch (start us, length us, event | category | flops | bytes accessed | tf_op | source)
XLA Modules:
  0.0 889.2 jit_solution(9244973140419626616)
XLA Ops:
  6.5 26.0 %copy.35 = bf16[1,2048,3584]{2,0,1:T(2,128)(2,1)} copy(bf16[1,2048,3584]{2,1,0:T(8,128)(2,1)} %param.4) | data formatting | bytes 29360128 | tf_op args[0]
  33.1 94.1 %reduce.36 = bf16[2048,3584]{1,0:T(8,128)(2,1)} reduce(bf16[2048,1,3584]{2,1,0:T(2,128)(2,1)} %bitcast.244, bf16[]{:T(256)} %broadcast.509), dimensions={1}, to_apply=%bitcast.229.reduce_sub_computation | reduce | bytes 29360130
  127.2 16.2 %reshape.534 = bf16[8,2,458752]{2,1,0:T(2,128)(2,1)} reshape(bf16[2048,3584]{1,0:T(8,128)(2,1)} %reduce.36) | data formatting | bytes 29360128
  143.5 5.6 all-to-all-start
  149.9 161.3 %all-to-all-done = bf16[8,2,458752]{2,1,0:T(2,128)(2,1)} async-done(((bf16[8,2,458752]{2,1,0:T(2,128)(2,1)}), bf16[8,2,458752]{2,1,0:T(2,128)(2,1)}, u32[]{:S(2)}, u32[]{:S(2)}) %all-to-all-start) | async-done | bytes 14680096 | tf_op jit(solution)/shard_map/all_to_all | solution.py:27
  311.2 20.2 %reshape.535 = bf16[2048,1,3584]{2,1,0:T(2,128)(2,1)} reshape(bf16[8,2,458752]{2,1,0:T(2,128)(2,1)} %all-to-all-done) | data formatting | bytes 29360128
  331.4 19.4 %copy.33 = bf16[1,2048,3584]{2,1,0:T(8,128)(2,1)} copy(bf16[1,2048,3584]{2,0,1:T(2,128)(2,1)} %bitcast.245) | data formatting | bytes 29360128
  350.8 18.7 %copy.25 = bf16[1,256,8,3584]{1,3,2,0:T(8,128)(2,1)} copy(bf16[1,256,8,3584]{3,1,2,0:T(8,128)(2,1)} %bitcast.246) | data formatting | bytes 29360128 | tf_op jit(solution)/shard_map/all_to_all | solution.py:27
  369.5 42.8 %while.18 = (s32[]{:T(128)}, f32[256,1,512]{0,2,1:T(8,128)S(1)}, s32[1]{0:T(128)}, bf16[1,256,28672]{1,2,0:T(8,128)(2,1)}, s32[]{:T(128)}, /*index=5*/s32[]{:T(128)}, s32[]{:T(128)}, s32[]{:T(128)}) while((s32[]{:T(128)}, f32[256,1,512]{0,2,1:T(8,128)S(1)}, s32[1]{0:T(128)}, bf16[1,256,28672]{1,2,0:T(8,128)(2,1)}, s32[]{:T(128)}, ...), condition=%wide.region_1.0_spmd.clone, body=%wide.region_0.0_spmd.clone.sunk | while | flops 963648512 | bytes 2912925 | solution.py:36
  374.8 5.3 fusion.119
  415.8 129.5 %all-reduce.3.cloned.1.call-done = f32[1,512,512]{1,2,0:T(8,128)} async-done(((f32[1,512,512]{1,2,0:T(8,128)}), f32[1,512,512]{1,2,0:T(8,128)}) %all-reduce.3.cloned.1.call-update) | async-done | bytes 1048592 | tf_op jit(solution)/shard_map/psum | solution.py:46
  548.4 11.7 %custom-call.34 = f32[1,128,128]{2,1,0:T(8,128)S(1)} custom-call(f32[1,128,128]{2,1,0:T(8,128)S(1)} %cholesky.267), custom_call_target="Cholesky" | custom-call | tf_op jit(solution)/shard_map/jit(cholesky)/cholesky | solution.py:47
  560.1 9.8 %custom-call.35 = f32[1,1,128,128]{2,3,1,0:T(8,128)S(1)} custom-call(f32[1,1,128,128]{3,2,1,0:T(8,128)S(1)} %get-tuple-element.179), custom_call_target="InvertDiagBlocksLowerTriangular" | custom-call | tf_op jit(solution)/shard_map/jit(cholesky)/cholesky | solution.py:47
  570.7 11.7 %custom-call.36 = f32[1,128,128]{2,1,0:T(8,128)S(1)} custom-call(f32[1,128,128]{2,1,0:T(8,128)S(1)} %cholesky.271), custom_call_target="Cholesky" | custom-call | tf_op jit(solution)/shard_map/jit(cholesky)/cholesky | solution.py:47
  582.5 10.2 %custom-call.37 = f32[1,1,128,128]{2,3,1,0:T(8,128)S(1)} custom-call(f32[1,1,128,128]{3,2,1,0:T(8,128)S(1)} %get-tuple-element.176), custom_call_target="InvertDiagBlocksLowerTriangular" | custom-call | tf_op jit(solution)/shard_map/jit(cholesky)/cholesky | solution.py:47
  593.4 11.7 %custom-call.38 = f32[1,128,128]{2,1,0:T(8,128)S(1)} custom-call(f32[1,128,128]{2,1,0:T(8,128)S(1)} %cholesky.276), custom_call_target="Cholesky" | custom-call | tf_op jit(solution)/shard_map/jit(cholesky)/cholesky | solution.py:47
  605.8 9.8 %custom-call.39 = f32[1,1,128,128]{2,3,1,0:T(8,128)S(1)} custom-call(f32[1,1,128,128]{3,2,1,0:T(8,128)S(1)} %get-tuple-element.173), custom_call_target="InvertDiagBlocksLowerTriangular" | custom-call | tf_op jit(solution)/shard_map/jit(cholesky)/cholesky | solution.py:47
  616.2 11.9 %custom-call.40 = f32[1,128,128]{2,1,0:T(8,128)S(1)} custom-call(f32[1,128,128]{2,1,0:T(8,128)S(1)} %fusion.62), custom_call_target="Cholesky" | custom-call | tf_op jit(solution)/shard_map/jit(cholesky)/cholesky | solution.py:47
  632.0 10.5 %while.17 = (s32[]{:T(128)}, f32[1,512,512]{2,1,0:T(8,128)S(1)}, s32[4,2]{0,1:T(2,128)S(1)}, f32[4,1,128,128]{3,2,1,0:T(8,128)}, s32[]{:T(128)}) while((s32[]{:T(128)}, f32[1,512,512]{2,1,0:T(8,128)S(1)}, s32[4,2]{0,1:T(2,128)S(1)}, f32[4,1,128,128]{3,2,1,0:T(8,128)}, s32[]{:T(128)}) %tuple.72), condition=%wide.while_cond, body=%wide.while_body.sunk | while | flops 2 | bytes 132205 | solution.py:49
  642.5 40.1 %custom-call.41 = f32[1,4,128,128]{2,3,1,0:T(8,128)S(1)} custom-call(f32[1,4,128,128]{3,2,1,0:T(8,128)} %bitcast.261), custom_call_target="InvertDiagBlocksLowerTriangular" | custom-call | tf_op jit(solution)/shard_map/triangular_solve | solution.py:49
  692.1 5.8 fusion.42
  700.6 5.7 fusion.40
  729.9 21.0 %add_bitcast_fusion = f32[512,1,3584]{0,2,1:T(8,128)} fusion(f32[3584,512]{1,0:T(8,128)} %fusion.30, f32[3584,512]{1,0:T(8,128)} %fusion.32, f32[3584,512]{1,0:T(8,128)} %fusion.34, f32[3584,512]{1,0:T(8,128)} %fusion.36, f32[3584,512]{1,0:T(8,128)} %fusion.38, f32[3584,512]{1,0:T(8,128)} %fusion.42, f32[3584,512]{1,0:T(8,128)} %fusion.40, ...), kind=kOutput, calls=%fused_computation.25 | convolution fusion | flops 952369152 | bytes 60817412 | tf_op jit(solution)/shard_map/mdr,mdc->rmc/dot_general | solution.py:79
  751.0 128.3 %reduce-scatter.2.cloned.1.call-done = f32[128,1,3584]{0,2,1:T(8,128)} async-done(((f32[512,1,3584]{0,2,1:T(8,128)}), f32[128,1,3584]{0,2,1:T(8,128)}) %reduce-scatter.2.cloned.1.call-update) | async-done | bytes 1835024 | tf_op jit(solution)/shard_map/reduce_scatter | solution.py:89
  (96 shorter events, 97.7 us)
Async XLA Ops:
  143.5 167.7 %all-to-all-start = ((bf16[8,2,458752]{2,1,0:T(2,128)(2,1)}), bf16[8,2,458752]{2,1,0:T(2,128)(2,1)}, u32[]{:S(2)}, u32[]{:S(2)}) async-start(bf16[8,2,458752]{2,1,0:T(2,128)(2,1)} %reshape.534), calls=%async_computation | async-start | bytes 29360128 | tf_op jit(solution)/shard_map/all_to_all | solution.py:27
  149.0 396.3 %all-reduce.3.cloned.1.call-start = ((), (), s32[]{:S(2)}) async-start(), calls=%async_computation.2 | async-start | bytes 2097152 | tf_op jit(solution)/shard_map/psum | solution.py:46
  414.4 464.9 %reduce-scatter.2.cloned.1.call-start = ((), (), s32[]{:S(2)}) async-start(), calls=%async_computation.3 | async-start | bytes 9175040 | tf_op jit(solution)/shard_map/reduce_scatter | solution.py:89
  632.0 74.2 %slice-start = ((s8[14680064]{0:T(1024)(128)(4,1)}), s8[2097152]{0:T(1024)(128)(4,1)S(1)}, s32[]{:S(2)}) async-start(s8[14680064]{0:T(1024)(128)(4,1)} %bitcast.247), calls=%async_computation.4 | async-start | bytes 4194304
  689.4 8.5 collective-permute-start.1
  689.5 8.4 collective-permute-start
  692.1 14.1 %slice-start.1 = ((s8[14680064]{0:T(1024)(128)(4,1)}), s8[4194304]{0:T(1024)(128)(4,1)S(1)}, s32[]{:S(2)}) async-start(s8[14680064]{0:T(1024)(128)(4,1)} %bitcast.247), calls=%async_computation.5 | async-start | bytes 8388608
  692.1 14.1 %slice-start.2 = ((s8[14680064]{0:T(1024)(128)(4,1)}), s8[4194304]{0:T(1024)(128)(4,1)S(1)}, s32[]{:S(2)}) async-start(s8[14680064]{0:T(1024)(128)(4,1)} %bitcast.247), calls=%async_computation.6 | async-start | bytes 8388608
  697.9 8.3 slice-start.3
  697.9 12.4 %collective-permute-start.3 = (bf16[1,256,512]{1,2,0:T(8,128)(2,1)S(1)}, bf16[1,256,512]{1,2,0:T(8,128)(2,1)S(1)}, u32[]{:S(2)}, u32[]{:S(2)}) collective-permute-start(bf16[1,256,512]{1,2,0:T(8,128)(2,1)S(1)} %collective-permute-done.1), channel_id=1, source_target_pairs={{0,1},{1,2},{2,3},{3,4},{4,5},{5,6},{6,7},{7,0},{8,9},{9,10},{10,1... | collective-permute-start | bytes 786440 | tf_op jit(solution)/shard_map/ppermute | solution.py:67
  697.9 12.4 %collective-permute-start.2 = (bf16[1,256,512]{1,2,0:T(8,128)(2,1)S(1)}, bf16[1,256,512]{1,2,0:T(8,128)(2,1)S(1)}, u32[]{:S(2)}, u32[]{:S(2)}) collective-permute-start(bf16[1,256,512]{1,2,0:T(8,128)(2,1)S(1)} %collective-permute-done), channel_id=1, source_target_pairs={{0,7},{1,0},{2,1},{3,2},{4,3},{5,4},{6,5},{7,6},{8,15},{9,8},{10,9... | collective-permute-start | bytes 786440 | tf_op jit(solution)/shard_map/ppermute | solution.py:69
  710.4 11.0 %collective-permute-start.5 = (bf16[1,256,512]{1,2,0:T(8,128)(2,1)S(1)}, bf16[1,256,512]{1,2,0:T(8,128)(2,1)S(1)}, u32[]{:S(2)}, u32[]{:S(2)}) collective-permute-start(bf16[1,256,512]{1,2,0:T(8,128)(2,1)S(1)} %collective-permute-done.3), channel_id=1, source_target_pairs={{0,1},{1,2},{2,3},{3,4},{4,5},{5,6},{6,7},{7,0},{8,9},{9,10},{10,1... | collective-permute-start | bytes 786440 | tf_op jit(solution)/shard_map/ppermute | solution.py:67
  710.4 15.3 %collective-permute-start.4 = (bf16[1,256,512]{1,2,0:T(8,128)(2,1)S(1)}, bf16[1,256,512]{1,2,0:T(8,128)(2,1)S(1)}, u32[]{:S(2)}, u32[]{:S(2)}) collective-permute-start(bf16[1,256,512]{1,2,0:T(8,128)(2,1)S(1)} %collective-permute-done.2), channel_id=1, source_target_pairs={{0,7},{1,0},{2,1},{3,2},{4,3},{5,4},{6,5},{7,6},{8,15},{9,8},{10,9... | collective-permute-start | bytes 786440 | tf_op jit(solution)/shard_map/ppermute | solution.py:69
  721.3 8.6 collective-permute-start.6
Sparse Core Ops, SparseCore 0:
  414.5 130.7 all-reduce.2
  751.1 128.1 reduce-scatter.1
